TPU v7x, 128 devices: a whole 4x4x4 slice. The times are simulated.
128 devices in a mesh: dp: 16 (over x, z), fsdp: 8 (over y, core).
Axes of the slice: x: 4, y: 4, z: 4, core: 2. Of those that a mesh axis runs over, the one named last changes fastest.
Arguments:
- tokens: bfloat16 [2048, 4096], P('dp', 'fsdp'), may hold values from -6 to 6
- expert_ids: int32 [2048, 2], P('dp'), may hold values from 0 to 7, all different within a row; in each aligned block of 128 rows (0 to 127, 128 to 255, ...) at most 40 rows name the same one
- route_probs: float32 [2048, 2], P('dp'), may hold values from 0.1 to 0.9
- w_gate: bfloat16 [4096, 65536], P(None, ('dp', 'fsdp')), may hold values from -0.09375 to 0.09375
- w_up: bfloat16 [4096, 65536], P(None, ('dp', 'fsdp')), may hold values from -0.09375 to 0.09375
- w_down: bfloat16 [65536, 4096], P(('dp', 'fsdp')), may hold values from -0.0625 to 0.0625
- out_grad: bfloat16 [2048, 4096], P('dp', 'fsdp'), may hold values from -0.59765625 to 0.59765625
Outputs:
- mixed: bfloat16 [2048, 4096], P('dp', 'fsdp')
- token_grad: bfloat16 [2048, 4096], P('dp', 'fsdp')
- prob_grad: float32 [2048, 2], P('dp')
- gate_weight_grad: bfloat16 [4096, 65536], P(None, ('dp', 'fsdp'))
- up_weight_grad: bfloat16 [4096, 65536], P(None, ('dp', 'fsdp'))
- down_weight_grad: bfloat16 [65536, 4096], P(('dp', 'fsdp'))
Inputs may be any that keep to these rules, and one draw needn't show every extreme that they name: `expert_ids`: each token names two different experts. Within the 128 tokens of one dp index (aligned blocks of rows) no expert is named more than 40 times, and in some block one expert is named exactly 40 times.
All inputs are finite; a program needn't handle non-finite values.
Results may differ from a plain program's by a relative error of at most 0.019.
Values may be sent and summed in bfloat16 or wider, within the bound.
No kernel may reach another device: no remote copies, remote signals or barrier semaphores. Data moves between devices by JAX's collectives and lax.ppermute only.
A program may use at most 128 MiB of HBM per device.

v0:
```python
import jax
import jax.numpy as jnp
from jax import lax
from jax.sharding import PartitionSpec as P

E = 8
CAP = 40


def local(tokens, expert_ids, route_probs, w_gate, w_up, w_down, out_grad):
    dp_count = lax.axis_size("dp")
    groups = dp_count // E
    token_count = tokens.shape[0]
    slot_total = E * CAP
    routing = expert_ids.reshape(-1)
    onehot = (routing[:, None] == jnp.arange(E, dtype=jnp.int32)[None, :]).astype(jnp.int32)
    position = jnp.sum((jnp.cumsum(onehot, axis=0) - onehot) * onehot, axis=1)
    slot_of = (routing * CAP + position).reshape(token_count, 2)
    slot_index = jnp.arange(slot_total, dtype=jnp.int32)
    select_first = slot_of[:, 0:1] == slot_index[None, :]
    select_second = slot_of[:, 1:2] == slot_index[None, :]
    picker = jnp.logical_or(select_first, select_second)
    picker_bf = picker.astype(jnp.bfloat16)
    weighted = jnp.where(select_first, route_probs[:, 0:1], 0.0) + jnp.where(
        select_second, route_probs[:, 1:2], 0.0
    )
    contract_rows = (((0,), (0,)), ((), ()))
    back_dims = (((1,), (1,)), ((), ()))

    def place_rows(source, scaled):
        if scaled:
            placed = lax.dot_general(
                weighted,
                source.astype(jnp.float32),
                contract_rows,
                precision=lax.Precision.HIGHEST,
                preferred_element_type=jnp.float32,
            )
        else:
            placed = lax.dot_general(
                picker_bf, source, contract_rows, preferred_element_type=jnp.float32
            )
        placed = placed.astype(jnp.bfloat16).reshape(E, CAP, source.shape[1])
        return jnp.repeat(placed, groups, axis=0)

    def to_expert_layout(source, scaled):
        joined = lax.all_gather(source, "fsdp", axis=1, tiled=True)
        arrived = lax.all_to_all(
            place_rows(joined, scaled), "dp", split_axis=0, concat_axis=0, tiled=True
        )
        return arrived.reshape(dp_count * CAP, arrived.shape[2])

    def to_token_layout(partial_value):
        shares = lax.psum_scatter(
            partial_value.astype(jnp.bfloat16), "fsdp", scatter_dimension=1, tiled=True
        ).astype(jnp.float32)
        returned = lax.all_to_all(
            shares.reshape(dp_count, CAP, shares.shape[1]).astype(jnp.bfloat16),
            "dp",
            split_axis=0,
            concat_axis=0,
            tiled=True,
        ).astype(jnp.float32)
        return jnp.sum(returned.reshape(E, groups, CAP, returned.shape[2]), axis=1).reshape(
            slot_total, returned.shape[2]
        )

    expert_rows = to_expert_layout(tokens, False)
    gate_proj = jnp.dot(expert_rows, w_gate, preferred_element_type=jnp.float32)
    up_proj = jnp.dot(expert_rows, w_up, preferred_element_type=jnp.float32)
    sigmoid_gate = jax.nn.sigmoid(gate_proj)
    activated = gate_proj * sigmoid_gate
    hidden = (activated * up_proj).astype(jnp.bfloat16)
    out_partial = jnp.dot(hidden, w_down, preferred_element_type=jnp.float32)
    out_slots = to_token_layout(out_partial)
    first_pair = jnp.dot(
        select_first.astype(jnp.float32),
        out_slots,
        precision=lax.Precision.HIGHEST,
        preferred_element_type=jnp.float32,
    )
    second_pair = jnp.dot(
        select_second.astype(jnp.float32),
        out_slots,
        precision=lax.Precision.HIGHEST,
        preferred_element_type=jnp.float32,
    )
    mixed = (route_probs[:, 0:1] * first_pair + route_probs[:, 1:2] * second_pair).astype(
        jnp.bfloat16
    )
    grad_local = out_grad.astype(jnp.float32)
    prob_terms = jnp.stack(
        [jnp.sum(first_pair * grad_local, axis=1), jnp.sum(second_pair * grad_local, axis=1)],
        axis=1,
    )
    prob_grad = lax.psum(prob_terms, "fsdp")
    grad_rows = to_expert_layout(out_grad, True)
    hidden_grad = lax.dot_general(grad_rows, w_down, back_dims, preferred_element_type=jnp.float32)
    gate_grad = (
        hidden_grad * up_proj * sigmoid_gate * (1.0 + gate_proj * (1.0 - sigmoid_gate))
    ).astype(jnp.bfloat16)
    up_grad = (hidden_grad * activated).astype(jnp.bfloat16)
    gate_weight_grad = lax.dot_general(
        expert_rows, gate_grad, contract_rows, preferred_element_type=jnp.float32
    ).astype(jnp.bfloat16)
    up_weight_grad = lax.dot_general(
        expert_rows, up_grad, contract_rows, preferred_element_type=jnp.float32
    ).astype(jnp.bfloat16)
    down_weight_grad = lax.dot_general(
        hidden, grad_rows, contract_rows, preferred_element_type=jnp.float32
    ).astype(jnp.bfloat16)
    input_partial = lax.dot_general(
        gate_grad, w_gate, back_dims, preferred_element_type=jnp.float32
    )
    input_partial = input_partial + lax.dot_general(
        up_grad, w_up, back_dims, preferred_element_type=jnp.float32
    )
    input_slots = to_token_layout(input_partial)
    token_grad = jnp.dot(
        picker.astype(jnp.float32),
        input_slots,
        precision=lax.Precision.HIGHEST,
        preferred_element_type=jnp.float32,
    ).astype(jnp.bfloat16)
    return (mixed, token_grad, prob_grad, gate_weight_grad, up_weight_grad, down_weight_grad)


def solution(mesh):
    placed = (
        P("dp", "fsdp"),
        P("dp", None),
        P("dp", None),
        P(None, ("dp", "fsdp")),
        P(None, ("dp", "fsdp")),
        P(("dp", "fsdp"), None),
        P("dp", "fsdp"),
    )
    return jax.shard_map(
        local,
        mesh=mesh,
        in_specs=placed,
        out_specs=(
            P("dp", "fsdp"),
            P("dp", "fsdp"),
            P("dp", None),
            P(None, ("dp", "fsdp")),
            P(None, ("dp", "fsdp")),
            P(("dp", "fsdp"), None),
        ),
        check_vma=False,
    )
```

profile of v0, /device:TPU:2, one launch (start us, length us, event | category | flops | bytes accessed | tf_op | source)
XLA Modules:
  0.0 347.4 jit_solution(6366988755404527250)
XLA Ops:
  7.2 0.0 all-gather.3.cloned.1.call-start
  7.2 0.7 all-gather.3.cloned.1.call-update
  7.9 0.8 copy.21
  8.7 0.1 eq.59
  8.8 0.1 eq.55
  9.0 0.6 reduce-window.6
  9.6 0.2 slice_reduce_fusion
  9.8 0.1 fusion.23
  9.9 0.1 reduce_sum.48
  10.1 0.1 copy.23
  10.1 0.7 multiply_add_fusion
  10.8 24.6 %all-gather.3.cloned.1.call-done = bf16[128,4096]{1,0:T(8,128)(2,1)} async-done(((bf16[128,512]{1,0:T(8,128)(2,1)}), bf16[128,4096]{1,0:T(8,128)(2,1)}) %all-gather.3.cloned.1.call-update) | async-done | bytes 1048592 | tf_op jit(solution)/shard_map/all_gather | solution.py:47
  35.5 2.2 convolution_convert_fusion.5
  37.6 3.0 broadcast_in_dim.27
  40.6 0.0 copy-start.1
  40.6 7.5 %all-to-all-start = ((bf16[16,40,4096]{2,1,0:T(8,128)(2,1)}), bf16[16,40,4096]{2,1,0:T(8,128)(2,1)}, u32[]{:S(2)}, u32[]{:S(2)}) async-start(bf16[16,40,4096]{2,1,0:T(8,128)(2,1)} %bitcast.57), calls=%async_computation | async-start | bytes 10485760 | tf_op jit(solution)/shard_map/all_to_all | solution.py:48
  48.2 0.0 all-gather.5.cloned.1.call-start
  48.2 0.7 all-gather.5.cloned.1.call-update
  48.9 0.0 copy-done.1
  49.0 24.8 %all-gather.5.cloned.1.call-done = bf16[128,4096]{1,0:T(8,128)(2,1)} async-done(((bf16[128,512]{1,0:T(8,128)(2,1)}), bf16[128,4096]{1,0:T(8,128)(2,1)}) %all-gather.5.cloned.1.call-update) | async-done | bytes 1048592 | tf_op jit(solution)/shard_map/all_gather | solution.py:47
  73.8 3.6 %convolution_convert_fusion.4 = bf16[320,4096]{1,0:T(8,128)(2,1)S(1)} fusion(bf16[128,4096]{1,0:T(8,128)(2,1)} %all-gather.5.cloned.1.call-done, f32[128]{0:T(128)S(1)} %get-tuple-element.13, f32[128]{0:T(128)S(1)} %get-tuple-element.12, s32[128]{0:T(128)S(1)} %get-tuple-element.15, s32[128]{0:T(128)S(1)} %get-tuple-element.14), kind=kOutput, calls=%fused_computation.5 | convolution fusion | flops 2014781440 | bytes 3672064 | tf_op jit(solution)/shard_map/dot_general | solution.py:32
  77.4 38.4 %all-to-all-done = bf16[16,40,4096]{2,1,0:T(8,128)(2,1)} async-done(((bf16[16,40,4096]{2,1,0:T(8,128)(2,1)}), bf16[16,40,4096]{2,1,0:T(8,128)(2,1)}, u32[]{:S(2)}, u32[]{:S(2)}) %all-to-all-start) | async-done | bytes 5242912 | tf_op jit(solution)/shard_map/all_to_all | solution.py:48
  115.7 3.0 broadcast_in_dim.31
  118.7 24.0 %all-to-all-start.2 = ((bf16[16,40,4096]{2,1,0:T(8,128)(2,1)}), bf16[16,40,4096]{2,1,0:T(8,128)(2,1)}, u32[]{:S(2)}, u32[]{:S(2)}) async-start(bf16[16,40,4096]{2,1,0:T(8,128)(2,1)} %bitcast.58), calls=%async_computation.3 | async-start | bytes 10485760 | tf_op jit(solution)/shard_map/all_to_all | solution.py:48
  142.7 0.2 reduce-scatter.3.cloned.1.call-start
  142.9 0.0 copy-start.3
  143.0 7.8 %fusion.26 = f32[640,512]{1,0:T(8,128)} fusion(bf16[640,4096]{1,0:T(8,128)(2,1)} %bitcast.7, bf16[4096,512]{1,0:T(8,128)(2,1)} %param.10), kind=kOutput, calls=%fused_computation.53 | convolution fusion | flops 2684354560 | bytes 10747904 | tf_op jit(solution)/shard_map/dot_general | solution.py:69
  150.8 0.0 copy-done.3
  150.8 6.4 %fusion.27 = f32[640,512]{1,0:T(8,128)} fusion(bf16[640,4096]{1,0:T(8,128)(2,1)} %bitcast.7, bf16[4096,512]{1,0:T(8,128)(2,1)S(1)} %copy-done.3), kind=kOutput, calls=%fused_computation.54 | convolution fusion | flops 2684354560 | bytes 10747904 | tf_op jit(solution)/shard_map/dot_general | solution.py:70
  157.2 53.1 %all-to-all-done.2 = bf16[16,40,4096]{2,1,0:T(8,128)(2,1)} async-done(((bf16[16,40,4096]{2,1,0:T(8,128)(2,1)}), bf16[16,40,4096]{2,1,0:T(8,128)(2,1)}, u32[]{:S(2)}, u32[]{:S(2)}) %all-to-all-start.2) | async-done | bytes 5242912 | tf_op jit(solution)/shard_map/all_to_all | solution.py:48
  210.3 0.0 copy-start.2
  210.3 8.0 %multiply_convert_fusion = (bf16[640,512]{1,0:T(8,128)(2,1)S(1)}, bf16[640,512]{1,0:T(8,128)(2,1)S(1)}, bf16[640,512]{1,0:T(8,128)(2,1)S(1)}) fusion(f32[640,512]{1,0:T(8,128)} %fusion.26, f32[640,512]{1,0:T(8,128)} %fusion.27, bf16[640,4096]{1,0:T(8,128)(2,1)} %bitcast.14, bf16[512,4096]{1,0:T(8,128)(2,1)} %param.12), kind=kOutput, calls=%fused_computation.9 | convolution fusion | flops 2689269760 | bytes 14024704 | tf_op jit(solution)/shard_map/dot_general | solution.py:98
  218.3 0.0 copy-done.2
  218.3 4.7 %convolution_convert_fusion = bf16[640,4096]{1,0:T(8,128)(2,1)} fusion(bf16[640,512]{1,0:T(8,128)(2,1)S(1)} %get-tuple-element.10, bf16[512,4096]{1,0:T(8,128)(2,1)S(1)} %copy-done.2), kind=kOutput, calls=%fused_computation.1 | convolution fusion | flops 2686976000 | bytes 10092544 | tf_op jit(solution)/shard_map/dot_general | solution.py:74
  223.0 0.0 reduce-scatter.3.cloned.1.call-update
  223.0 0.3 reduce-scatter.5.cloned.1.call-start
  223.3 0.0 copy-start.4
  223.3 4.9 %fusion.28 = f32[640,4096]{1,0:T(8,128)S(1)} fusion(bf16[640,512]{1,0:T(8,128)(2,1)S(1)} %get-tuple-element.9, bf16[4096,512]{1,0:T(8,128)(2,1)} %param.10), kind=kOutput, calls=%fused_computation.55 | convolution fusion | flops 2684354560 | bytes 15335424 | tf_op jit(solution)/shard_map/dot_general | solution.py:112
  228.2 0.0 copy-done.4
  228.2 4.8 %add_convert_fusion = bf16[640,4096]{1,0:T(8,128)(2,1)} fusion(f32[640,4096]{1,0:T(8,128)S(1)} %fusion.28, bf16[640,512]{1,0:T(8,128)(2,1)S(1)} %get-tuple-element.8, bf16[4096,512]{1,0:T(8,128)(2,1)S(1)} %copy-done.4), kind=kOutput, calls=%fused_computation | convolution fusion | flops 2689597440 | bytes 20578304 | tf_op jit(solution)/shard_map/dot_general | solution.py:115
  232.9 0.0 reduce-scatter.5.cloned.1.call-update
  233.0 7.5 %convolution_convert_fusion.1 = bf16[512,4096]{1,0:T(8,128)(2,1)} fusion(bf16[640,512]{1,0:T(8,128)(2,1)S(1)} %get-tuple-element.10, bf16[640,4096]{1,0:T(8,128)(2,1)} %bitcast.14), kind=kOutput, calls=%fused_computation.2 | convolution fusion | flops 2686451712 | bytes 10092544 | tf_op jit(solution)/shard_map/dot_general | solution.py:109
  240.5 7.5 %convolution_convert_fusion.2 = bf16[4096,512]{1,0:T(8,128)(2,1)} fusion(bf16[640,4096]{1,0:T(8,128)(2,1)} %bitcast.7, bf16[640,512]{1,0:T(8,128)(2,1)S(1)} %get-tuple-element.8), kind=kOutput, calls=%fused_computation.3 | convolution fusion | flops 2686451712 | bytes 10092544 | tf_op jit(solution)/shard_map/dot_general | solution.py:106
  248.0 26.8 %reduce-scatter.3.cloned.1.call-done = bf16[640,512]{1,0:T(8,128)(2,1)} async-done(((bf16[640,4096]{1,0:T(8,128)(2,1)}), bf16[640,512]{1,0:T(8,128)(2,1)}) %reduce-scatter.3.cloned.1.call-update) | async-done | bytes 655376 | tf_op jit(solution)/shard_map/reduce_scatter | solution.py:54
  274.8 7.5 %all-to-all-start.1 = ((bf16[16,40,512]{2,1,0:T(8,128)(2,1)}), bf16[16,40,512]{2,1,0:T(8,128)(2,1)S(1)}, u32[]{:S(2)}, u32[]{:S(2)}) async-start(bf16[16,40,512]{2,1,0:T(8,128)(2,1)} %bitcast.65), calls=%async_computation.2 | async-start | bytes 1310720 | tf_op jit(solution)/shard_map/all_to_all | solution.py:57
  282.2 0.0 copy-start
  282.3 7.6 %convolution_convert_fusion.3 = bf16[4096,512]{1,0:T(8,128)(2,1)} fusion(bf16[640,4096]{1,0:T(8,128)(2,1)} %bitcast.7, bf16[640,512]{1,0:T(8,128)(2,1)S(1)} %get-tuple-element.9), kind=kOutput, calls=%fused_computation.4 | convolution fusion | flops 2686451712 | bytes 10092544 | tf_op jit(solution)/shard_map/dot_general | solution.py:103
  289.9 26.6 %reduce-scatter.5.cloned.1.call-done = bf16[640,512]{1,0:T(8,128)(2,1)} async-done(((bf16[640,4096]{1,0:T(8,128)(2,1)}), bf16[640,512]{1,0:T(8,128)(2,1)}) %reduce-scatter.5.cloned.1.call-update) | async-done | bytes 655376 | tf_op jit(solution)/shard_map/reduce_scatter | solution.py:54
  316.5 0.0 all-to-all-done.1
  316.5 7.5 %all-to-all-start.3 = ((bf16[16,40,512]{2,1,0:T(8,128)(2,1)}), bf16[16,40,512]{2,1,0:T(8,128)(2,1)S(1)}, u32[]{:S(2)}, u32[]{:S(2)}) async-start(bf16[16,40,512]{2,1,0:T(8,128)(2,1)} %bitcast.64), calls=%async_computation.5 | async-start | bytes 1310720 | tf_op jit(solution)/shard_map/all_to_all | solution.py:57
  324.0 0.1 convert_reduce_fusion.1
  324.1 0.5 fusion.6
  324.5 0.0 copy-done
  324.6 1.1 fusion.1
  325.7 13.9 %psum.7 = f32[128,2]{0,1:T(2,128)} all-reduce(f32[128,2]{0,1:T(2,128)S(1)} %pad_maximum_fusion), channel_id=1, replica_groups=mesh['dp'=16,'fsdp'=8] {'fsdp'}, use_global_device_ids=true, to_apply=%region_9.10 | all-reduce | flops 256 | bytes 2048 | tf_op jit(solution)/shard_map/psum | solution.py:96
  339.6 0.0 all-to-all-done.3
  339.6 0.1 convert_reduce_fusion
  339.7 1.1 convolution_convert_fusion.6
  (6 shorter events, 0.1 us)
Async XLA Ops:
  7.2 28.3 %all-gather.3.cloned.1.call-start = ((), (), s32[]{:S(2)}) async-start(), calls=%async_computation.6 | async-start | bytes 1179648 | tf_op jit(solution)/shard_map/all_gather | solution.py:47
  40.6 8.3 %copy-start.1 = (f32[128,2]{0,1:T(2,128)S(1)}, f32[128,2]{0,1:T(2,128)}, u32[]{:S(2)}) copy-start(f32[128,2]{0,1:T(2,128)} %param.9) | copy-start | bytes 3076
  40.6 75.1 %all-to-all-start = ((bf16[16,40,4096]{2,1,0:T(8,128)(2,1)}), bf16[16,40,4096]{2,1,0:T(8,128)(2,1)}, u32[]{:S(2)}, u32[]{:S(2)}) async-start(bf16[16,40,4096]{2,1,0:T(8,128)(2,1)} %bitcast.57), calls=%async_computation | async-start | bytes 10485760 | tf_op jit(solution)/shard_map/all_to_all | solution.py:48
  48.2 25.6 %all-gather.5.cloned.1.call-start = ((), (), s32[]{:S(2)}) async-start(), calls=%async_computation.8 | async-start | bytes 1179648 | tf_op jit(solution)/shard_map/all_gather | solution.py:47
  118.7 91.6 %all-to-all-start.2 = ((bf16[16,40,4096]{2,1,0:T(8,128)(2,1)}), bf16[16,40,4096]{2,1,0:T(8,128)(2,1)}, u32[]{:S(2)}, u32[]{:S(2)}) async-start(bf16[16,40,4096]{2,1,0:T(8,128)(2,1)} %bitcast.58), calls=%async_computation.3 | async-start | bytes 10485760 | tf_op jit(solution)/shard_map/all_to_all | solution.py:48
  142.7 132.1 %reduce-scatter.3.cloned.1.call-start = ((), (), s32[]{:S(2)}) async-start(), calls=%async_computation.7 | async-start | bytes 5898240 | tf_op jit(solution)/shard_map/reduce_scatter | solution.py:54
  142.9 7.8 %copy-start.3 = (bf16[4096,512]{1,0:T(8,128)(2,1)S(1)}, bf16[4096,512]{1,0:T(8,128)(2,1)}, u32[]{:S(2)}) copy-start(bf16[4096,512]{1,0:T(8,128)(2,1)} %param.11) | copy-start | bytes 12582916
  210.3 8.0 %copy-start.2 = (bf16[512,4096]{1,0:T(8,128)(2,1)S(1)}, bf16[512,4096]{1,0:T(8,128)(2,1)}, u32[]{:S(2)}) copy-start(bf16[512,4096]{1,0:T(8,128)(2,1)} %param.12) | copy-start | bytes 12582916
  223.0 93.5 %reduce-scatter.5.cloned.1.call-start = ((), (), s32[]{:S(2)}) async-start(), calls=%async_computation.9 | async-start | bytes 5898240 | tf_op jit(solution)/shard_map/reduce_scatter | solution.py:54
  223.3 4.9 %copy-start.4 = (bf16[4096,512]{1,0:T(8,128)(2,1)S(1)}, bf16[4096,512]{1,0:T(8,128)(2,1)}, u32[]{:S(2)}) copy-start(bf16[4096,512]{1,0:T(8,128)(2,1)} %param.11) | copy-start | bytes 12582916
  274.8 41.7 %all-to-all-start.1 = ((bf16[16,40,512]{2,1,0:T(8,128)(2,1)}), bf16[16,40,512]{2,1,0:T(8,128)(2,1)S(1)}, u32[]{:S(2)}, u32[]{:S(2)}) async-start(bf16[16,40,512]{2,1,0:T(8,128)(2,1)} %bitcast.65), calls=%async_computation.2 | async-start | bytes 1310720 | tf_op jit(solution)/shard_map/all_to_all | solution.py:57
  282.2 42.3 %copy-start = (bf16[128,512]{1,0:T(8,128)(2,1)S(1)}, bf16[128,512]{1,0:T(8,128)(2,1)}, u32[]{:S(2)}) copy-start(bf16[128,512]{1,0:T(8,128)(2,1)} %param.13) | copy-start | bytes 393220
  316.5 23.1 %all-to-all-start.3 = ((bf16[16,40,512]{2,1,0:T(8,128)(2,1)}), bf16[16,40,512]{2,1,0:T(8,128)(2,1)S(1)}, u32[]{:S(2)}, u32[]{:S(2)}) async-start(bf16[16,40,512]{2,1,0:T(8,128)(2,1)} %bitcast.64), calls=%async_computation.5 | async-start | bytes 1310720 | tf_op jit(solution)/shard_map/all_to_all | solution.py:57
Sparse Core Ops, SparseCore 0:
  9.7 25.7 all-gather.2
  50.7 23.0 all-gather.4
  223.1 51.6 reduce-scatter.2
  277.0 39.3 reduce-scatter.4
where the time goes:
time: 348 us; the launch traced here: 347 us
  waiting for transfers between devices  196 us (56%)
  matrix products  67.6 us (19%)
  starting transfers between devices  47 us (14%)
  blocking collectives  13.9 us (4%)
  between operations  13.9 us (4%)
  local copies, waits for them, and re-layouts  7.52 us (2%)
    all_to_all x2, waiting for transfers between devices, to_expert_layout(): lax.all_to_all(place_rows(joined, scaled), 'dp', split_axis=0, concat_axi...  91.5 us
    reduce_scatter x2, waiting for transfers between devices, to_token_layout(): lax.psum_scatter(partial_value.astype(jnp.bfloat16), 'fsdp', scatter_dime...  53.4 us
    all_gather x2, waiting for transfers between devices, to_expert_layout(): joined = lax.all_gather(source, 'fsdp', axis=1, tiled=True)  49.5 us
    all_to_all x2, starting transfers between devices, to_expert_layout(): lax.all_to_all(place_rows(joined, scaled), 'dp', split_axis=0, concat_axi...  31.5 us
    all_to_all x2, starting transfers between devices, to_token_layout(): lax.all_to_all(shares.reshape(dp_count, CAP, shares.shape[1]).astype(jnp....  15 us
    psum x1, blocking collectives, local(): prob_grad = lax.psum(prob_terms, 'fsdp')  13.9 us
    dot_general x1, matrix products, local(): lax.dot_general(grad_rows, w_down, back_dims, preferred_element_type=jnp....  7.96 us
    dot_general x1, matrix products, local(): gate_proj = jnp.dot(expert_rows, w_gate, preferred_element_type=jnp.float32)  7.81 us
  transfers between devices with their start and end apart: 8, of which 6 were waited for; matrix products, arithmetic and copies ran while one was open for 16% of the time, Pallas kernels for 0%

commit v1 on v0

--- a/solution.py
+++ b/solution.py
@@ -5,6 +5,16 @@
 
 E = 8
 CAP = 40
+
+
+def gather_by_hops(array, mesh_axis, along):
+    size = lax.axis_size(mesh_axis)
+    block, tiles = (array, [array])
+    for _ in range(size - 1):
+        block = lax.ppermute(block, mesh_axis, [(i, (i + 1) % size) for i in range(size)])
+        tiles.insert(0, block)
+    line = jnp.concatenate(tiles, axis=along)
+    return jnp.roll(line, (lax.axis_index(mesh_axis) + 1) * array.shape[along], axis=along)
 
 
 def local(tokens, expert_ids, route_probs, w_gate, w_up, w_down, out_grad):
@@ -44,7 +54,7 @@
         return jnp.repeat(placed, groups, axis=0)
 
     def to_expert_layout(source, scaled):
-        joined = lax.all_gather(source, "fsdp", axis=1, tiled=True)
+        joined = gather_by_hops(source, "fsdp", 1)
         arrived = lax.all_to_all(
             place_rows(joined, scaled), "dp", split_axis=0, concat_axis=0, tiled=True
         )

time: 348 us -> 331 us (0.951)
  starting transfers between devices: 47 us -> 32.5 us
    ppermute x0 -> x14, waiting for transfers between devices: none -> 75.7 us  [gather_by_hops(): lax.ppermute(block, mesh_axis, [(i, (i + 1) % size) for i in range(size)])]
    all_gather x2 -> x0, waiting for transfers between devices: 49.5 us -> none  [to_expert_layout(): joined = lax.all_gather(source, 'fsdp', axis=1, tiled=True)]
    all_to_all x2, waiting for transfers between devices: 91.5 us -> 64.4 us  [to_expert_layout(): lax.all_to_all(place_rows(joined, scaled), 'dp', split_axis=0, concat_axi...]
    all_to_all x2, starting transfers between devices: 31.5 us -> 17.1 us  [to_expert_layout(): lax.all_to_all(place_rows(joined, scaled), 'dp', split_axis=0, concat_axi...]
  transfers between devices with their start and end apart: 8 -> 20, of which waited for: 6 -> 18; matrix products, arithmetic and copies ran while one was open for 16% -> 16% of each run, Pallas kernels for 0% -> 0%
where the time goes in v1:
time: 331 us; the launch traced here: 330 us
  waiting for transfers between devices  194 us (59%)
  matrix products  65.2 us (20%)
  starting transfers between devices  32.5 us (10%)
  between operations  14.3 us (4%)
  blocking collectives  13.9 us (4%)
  local copies, waits for them, and re-layouts  8.55 us (3%)
    ppermute x14, waiting for transfers between devices, gather_by_hops(): lax.ppermute(block, mesh_axis, [(i, (i + 1) % size) for i in range(size)])  75.7 us
    all_to_all x2, waiting for transfers between devices, to_expert_layout(): lax.all_to_all(place_rows(joined, scaled), 'dp', split_axis=0, concat_axi...  64.4 us
    reduce_scatter x2, waiting for transfers between devices, to_token_layout(): lax.psum_scatter(partial_value.astype(jnp.bfloat16), 'fsdp', scatter_dime...  53.8 us
    all_to_all x2, starting transfers between devices, to_expert_layout(): lax.all_to_all(place_rows(joined, scaled), 'dp', split_axis=0, concat_axi...  17.1 us
    all_to_all x2, starting transfers between devices, to_token_layout(): lax.all_to_all(shares.reshape(dp_count, CAP, shares.shape[1]).astype(jnp....  14.9 us
    psum x1, blocking collectives, local(): prob_grad = lax.psum(prob_terms, 'fsdp')  13.9 us
    dot_general x1, matrix products, local(): lax.dot_general(grad_rows, w_down, back_dims, preferred_element_type=jnp....  7.96 us
    dot_general x1, matrix products, local(): gate_proj = jnp.dot(expert_rows, w_gate, preferred_element_type=jnp.float32)  7.81 us
  transfers between devices with their start and end apart: 20, of which 18 were waited for; matrix products, arithmetic and copies ran while one was open for 16% of the time, Pallas kernels for 0%

profile of v1, /device:TPU:2, one launch (start us, length us, event | category | flops | bytes accessed | tf_op | source)
XLA Modules:
  0.0 329.9 jit_solution(3168089815974672454)
XLA Ops:
  7.2 0.0 collective-permute-start
  7.2 5.8 %collective-permute-done = bf16[128,512]{1,0:T(8,128)(2,1)S(1)} collective-permute-done((bf16[128,512]{1,0:T(8,128)(2,1)}, bf16[128,512]{1,0:T(8,128)(2,1)S(1)}, u32[]{:S(2)}, u32[]{:S(2)}) %collective-permute-start) | collective-permute-done | bytes 131104 | tf_op jit(solution)/shard_map/ppermute | solution.py:14
  13.0 0.0 collective-permute-start.1
  13.0 5.6 %collective-permute-done.1 = bf16[128,512]{1,0:T(8,128)(2,1)S(1)} collective-permute-done((bf16[128,512]{1,0:T(8,128)(2,1)S(1)}, bf16[128,512]{1,0:T(8,128)(2,1)S(1)}, u32[]{:S(2)}, u32[]{:S(2)}) %collective-permute-start.1) | collective-permute-done | bytes 131104 | tf_op jit(solution)/shard_map/ppermute | solution.py:14
  18.6 0.8 copy.21
  19.4 0.1 eq.61
  19.5 4.7 %collective-permute-done.2 = bf16[128,512]{1,0:T(8,128)(2,1)S(1)} collective-permute-done((bf16[128,512]{1,0:T(8,128)(2,1)S(1)}, bf16[128,512]{1,0:T(8,128)(2,1)S(1)}, u32[]{:S(2)}, u32[]{:S(2)}) %collective-permute-start.2) | collective-permute-done | bytes 131104 | tf_op jit(solution)/shard_map/ppermute | solution.py:14
  24.2 0.0 collective-permute-start.3
  24.2 0.6 reduce-window.6
  24.8 5.0 %collective-permute-done.3 = bf16[128,512]{1,0:T(8,128)(2,1)S(1)} collective-permute-done((bf16[128,512]{1,0:T(8,128)(2,1)S(1)}, bf16[128,512]{1,0:T(8,128)(2,1)S(1)}, u32[]{:S(2)}, u32[]{:S(2)}) %collective-permute-start.3) | collective-permute-done | bytes 131104 | tf_op jit(solution)/shard_map/ppermute | solution.py:14
  29.8 0.2 slice_reduce_fusion
  30.0 0.1 eq.57
  30.2 0.1 fusion.27
  30.3 0.1 reduce_sum.48
  30.5 0.1 copy.23
  30.5 4.9 %collective-permute-done.4 = bf16[128,512]{1,0:T(8,128)(2,1)S(1)} collective-permute-done((bf16[128,512]{1,0:T(8,128)(2,1)S(1)}, bf16[128,512]{1,0:T(8,128)(2,1)S(1)}, u32[]{:S(2)}, u32[]{:S(2)}) %collective-permute-start.4) | collective-permute-done | bytes 131104 | tf_op jit(solution)/shard_map/ppermute | solution.py:14
  35.4 0.0 collective-permute-start.5
  35.4 0.7 multiply_add_fusion
  36.1 4.9 %collective-permute-done.5 = bf16[128,512]{1,0:T(8,128)(2,1)S(1)} collective-permute-done((bf16[128,512]{1,0:T(8,128)(2,1)S(1)}, bf16[128,512]{1,0:T(8,128)(2,1)S(1)}, u32[]{:S(2)}, u32[]{:S(2)}) %collective-permute-start.5) | collective-permute-done | bytes 131104 | tf_op jit(solution)/shard_map/ppermute | solution.py:14
  41.0 5.6 %collective-permute-done.6 = bf16[128,512]{1,0:T(8,128)(2,1)S(1)} collective-permute-done((bf16[128,512]{1,0:T(8,128)(2,1)S(1)}, bf16[128,512]{1,0:T(8,128)(2,1)S(1)}, u32[]{:S(2)}, u32[]{:S(2)}) %collective-permute-start.6) | collective-permute-done | bytes 131104 | tf_op jit(solution)/shard_map/ppermute | solution.py:14
  46.7 0.9 constant_dynamic-update-slice_fusion
  47.7 1.0 convolution_convert_fusion.5
  48.6 3.0 broadcast_in_dim.27
  51.6 8.5 %all-to-all-start = ((bf16[16,40,4096]{2,1,0:T(8,128)(2,1)}), bf16[16,40,4096]{2,1,0:T(8,128)(2,1)}, u32[]{:S(2)}, u32[]{:S(2)}) async-start(bf16[16,40,4096]{2,1,0:T(8,128)(2,1)} %bitcast.55), calls=%async_computation | async-start | bytes 10485760 | tf_op jit(solution)/shard_map/all_to_all | solution.py:58
  60.1 0.0 collective-permute-start.7
  60.1 5.6 %collective-permute-done.7 = bf16[128,512]{1,0:T(8,128)(2,1)S(1)} collective-permute-done((bf16[128,512]{1,0:T(8,128)(2,1)S(1)}, bf16[128,512]{1,0:T(8,128)(2,1)S(1)}, u32[]{:S(2)}, u32[]{:S(2)}) %collective-permute-start.7) | collective-permute-done | bytes 131104 | tf_op jit(solution)/shard_map/ppermute | solution.py:14
  65.7 0.0 collective-permute-start.8
  65.7 5.6 %collective-permute-done.8 = bf16[128,512]{1,0:T(8,128)(2,1)S(1)} collective-permute-done((bf16[128,512]{1,0:T(8,128)(2,1)S(1)}, bf16[128,512]{1,0:T(8,128)(2,1)S(1)}, u32[]{:S(2)}, u32[]{:S(2)}) %collective-permute-start.8) | collective-permute-done | bytes 131104 | tf_op jit(solution)/shard_map/ppermute | solution.py:14
  71.3 5.6 %collective-permute-done.9 = bf16[128,512]{1,0:T(8,128)(2,1)S(1)} collective-permute-done((bf16[128,512]{1,0:T(8,128)(2,1)S(1)}, bf16[128,512]{1,0:T(8,128)(2,1)S(1)}, u32[]{:S(2)}, u32[]{:S(2)}) %collective-permute-start.9) | collective-permute-done | bytes 131104 | tf_op jit(solution)/shard_map/ppermute | solution.py:14
  76.9 0.0 collective-permute-start.10
  76.9 5.6 %collective-permute-done.10 = bf16[128,512]{1,0:T(8,128)(2,1)S(1)} collective-permute-done((bf16[128,512]{1,0:T(8,128)(2,1)S(1)}, bf16[128,512]{1,0:T(8,128)(2,1)S(1)}, u32[]{:S(2)}, u32[]{:S(2)}) %collective-permute-start.10) | collective-permute-done | bytes 131104 | tf_op jit(solution)/shard_map/ppermute | solution.py:14
  82.5 5.6 %collective-permute-done.11 = bf16[128,512]{1,0:T(8,128)(2,1)S(1)} collective-permute-done((bf16[128,512]{1,0:T(8,128)(2,1)S(1)}, bf16[128,512]{1,0:T(8,128)(2,1)S(1)}, u32[]{:S(2)}, u32[]{:S(2)}) %collective-permute-start.11) | collective-permute-done | bytes 131104 | tf_op jit(solution)/shard_map/ppermute | solution.py:14
  88.1 5.6 %collective-permute-done.12 = bf16[128,512]{1,0:T(8,128)(2,1)S(1)} collective-permute-done((bf16[128,512]{1,0:T(8,128)(2,1)S(1)}, bf16[128,512]{1,0:T(8,128)(2,1)S(1)}, u32[]{:S(2)}, u32[]{:S(2)}) %collective-permute-start.12) | collective-permute-done | bytes 131104 | tf_op jit(solution)/shard_map/ppermute | solution.py:14
  93.7 5.6 %collective-permute-done.13 = bf16[128,512]{1,0:T(8,128)(2,1)S(1)} collective-permute-done((bf16[128,512]{1,0:T(8,128)(2,1)S(1)}, bf16[128,512]{1,0:T(8,128)(2,1)S(1)}, u32[]{:S(2)}, u32[]{:S(2)}) %collective-permute-start.13) | collective-permute-done | bytes 131104 | tf_op jit(solution)/shard_map/ppermute | solution.py:14
  99.5 2.4 convolution_convert_fusion.4
  101.8 18.1 %all-to-all-done = bf16[16,40,4096]{2,1,0:T(8,128)(2,1)} async-done(((bf16[16,40,4096]{2,1,0:T(8,128)(2,1)}), bf16[16,40,4096]{2,1,0:T(8,128)(2,1)}, u32[]{:S(2)}, u32[]{:S(2)}) %all-to-all-start) | async-done | bytes 5242912 | tf_op jit(solution)/shard_map/all_to_all | solution.py:58
  120.0 3.0 broadcast_in_dim.31
  123.0 8.6 %all-to-all-start.2 = ((bf16[16,40,4096]{2,1,0:T(8,128)(2,1)}), bf16[16,40,4096]{2,1,0:T(8,128)(2,1)}, u32[]{:S(2)}, u32[]{:S(2)}) async-start(bf16[16,40,4096]{2,1,0:T(8,128)(2,1)} %bitcast.56), calls=%async_computation.3 | async-start | bytes 10485760 | tf_op jit(solution)/shard_map/all_to_all | solution.py:58
  131.6 0.2 reduce-scatter.3.cloned.1.call-start
  131.8 0.0 copy-start.3
  131.8 7.8 %fusion.34 = f32[640,512]{1,0:T(8,128)} fusion(bf16[640,4096]{1,0:T(8,128)(2,1)} %bitcast.7, bf16[4096,512]{1,0:T(8,128)(2,1)} %param.12), kind=kOutput, calls=%fused_computation.79 | convolution fusion | flops 2684354560 | bytes 10747904 | tf_op jit(solution)/shard_map/dot_general | solution.py:79
  139.6 6.4 %fusion.35 = f32[640,512]{1,0:T(8,128)} fusion(bf16[640,4096]{1,0:T(8,128)(2,1)} %bitcast.7, bf16[4096,512]{1,0:T(8,128)(2,1)S(1)} %copy-done.3), kind=kOutput, calls=%fused_computation.80 | convolution fusion | flops 2684354560 | bytes 10747904 | tf_op jit(solution)/shard_map/dot_general | solution.py:80
  146.1 46.3 %all-to-all-done.2 = bf16[16,40,4096]{2,1,0:T(8,128)(2,1)} async-done(((bf16[16,40,4096]{2,1,0:T(8,128)(2,1)}), bf16[16,40,4096]{2,1,0:T(8,128)(2,1)}, u32[]{:S(2)}, u32[]{:S(2)}) %all-to-all-start.2) | async-done | bytes 5242912 | tf_op jit(solution)/shard_map/all_to_all | solution.py:58
  192.3 8.0 %multiply_convert_fusion = (bf16[640,512]{1,0:T(8,128)(2,1)S(1)}, bf16[640,512]{1,0:T(8,128)(2,1)S(1)}, bf16[640,512]{1,0:T(8,128)(2,1)S(1)}) fusion(f32[640,512]{1,0:T(8,128)} %fusion.34, f32[640,512]{1,0:T(8,128)} %fusion.35, bf16[640,4096]{1,0:T(8,128)(2,1)} %bitcast.14, bf16[512,4096]{1,0:T(8,128)(2,1)} %param.14), kind=kOutput, calls=%fused_computation.13 | convolution fusion | flops 2689269760 | bytes 14024704 | tf_op jit(solution)/shard_map/dot_general | solution.py:108
  200.3 4.7 %convolution_convert_fusion = bf16[640,4096]{1,0:T(8,128)(2,1)} fusion(bf16[640,512]{1,0:T(8,128)(2,1)S(1)} %get-tuple-element.11, bf16[512,4096]{1,0:T(8,128)(2,1)S(1)} %copy-done.2), kind=kOutput, calls=%fused_computation.1 | convolution fusion | flops 2686976000 | bytes 10092544 | tf_op jit(solution)/shard_map/dot_general | solution.py:84
  205.0 0.0 reduce-scatter.3.cloned.1.call-update
  205.0 0.3 reduce-scatter.5.cloned.1.call-start
  205.3 0.0 copy-start.4
  205.3 4.9 %fusion.36 = f32[640,4096]{1,0:T(8,128)S(1)} fusion(bf16[640,512]{1,0:T(8,128)(2,1)S(1)} %get-tuple-element.10, bf16[4096,512]{1,0:T(8,128)(2,1)} %param.12), kind=kOutput, calls=%fused_computation.81 | convolution fusion | flops 2684354560 | bytes 15335424 | tf_op jit(solution)/shard_map/dot_general | solution.py:122
  210.2 4.7 %add_convert_fusion = bf16[640,4096]{1,0:T(8,128)(2,1)} fusion(f32[640,4096]{1,0:T(8,128)S(1)} %fusion.36, bf16[640,512]{1,0:T(8,128)(2,1)S(1)} %get-tuple-element.9, bf16[4096,512]{1,0:T(8,128)(2,1)S(1)} %copy-done.4), kind=kOutput, calls=%fused_computation | convolution fusion | flops 2689597440 | bytes 20578304 | tf_op jit(solution)/shard_map/dot_general | solution.py:125
  215.0 0.0 reduce-scatter.5.cloned.1.call-update
  215.0 7.5 %convolution_convert_fusion.1 = bf16[512,4096]{1,0:T(8,128)(2,1)} fusion(bf16[640,512]{1,0:T(8,128)(2,1)S(1)} %get-tuple-element.11, bf16[640,4096]{1,0:T(8,128)(2,1)} %bitcast.14), kind=kOutput, calls=%fused_computation.2 | convolution fusion | flops 2686451712 | bytes 10092544 | tf_op jit(solution)/shard_map/dot_general | solution.py:119
  222.5 7.5 %convolution_convert_fusion.2 = bf16[4096,512]{1,0:T(8,128)(2,1)} fusion(bf16[640,4096]{1,0:T(8,128)(2,1)} %bitcast.7, bf16[640,512]{1,0:T(8,128)(2,1)S(1)} %get-tuple-element.9), kind=kOutput, calls=%fused_computation.3 | convolution fusion | flops 2686451712 | bytes 10092544 | tf_op jit(solution)/shard_map/dot_general | solution.py:116
  230.0 27.0 %reduce-scatter.3.cloned.1.call-done = bf16[640,512]{1,0:T(8,128)(2,1)} async-done(((bf16[640,4096]{1,0:T(8,128)(2,1)}), bf16[640,512]{1,0:T(8,128)(2,1)}) %reduce-scatter.3.cloned.1.call-update) | async-done | bytes 655376 | tf_op jit(solution)/shard_map/reduce_scatter | solution.py:64
  257.0 7.4 %all-to-all-start.1 = ((bf16[16,40,512]{2,1,0:T(8,128)(2,1)}), bf16[16,40,512]{2,1,0:T(8,128)(2,1)S(1)}, u32[]{:S(2)}, u32[]{:S(2)}) async-start(bf16[16,40,512]{2,1,0:T(8,128)(2,1)} %bitcast.63), calls=%async_computation.2 | async-start | bytes 1310720 | tf_op jit(solution)/shard_map/all_to_all | solution.py:67
  264.5 7.6 %convolution_convert_fusion.3 = bf16[4096,512]{1,0:T(8,128)(2,1)} fusion(bf16[640,4096]{1,0:T(8,128)(2,1)} %bitcast.7, bf16[640,512]{1,0:T(8,128)(2,1)S(1)} %get-tuple-element.10), kind=kOutput, calls=%fused_computation.4 | convolution fusion | flops 2686451712 | bytes 10092544 | tf_op jit(solution)/shard_map/dot_general | solution.py:113
  272.0 26.8 %reduce-scatter.5.cloned.1.call-done = bf16[640,512]{1,0:T(8,128)(2,1)} async-done(((bf16[640,4096]{1,0:T(8,128)(2,1)}), bf16[640,512]{1,0:T(8,128)(2,1)}) %reduce-scatter.5.cloned.1.call-update) | async-done | bytes 655376 | tf_op jit(solution)/shard_map/reduce_scatter | solution.py:64
  298.9 7.4 %all-to-all-start.3 = ((bf16[16,40,512]{2,1,0:T(8,128)(2,1)}), bf16[16,40,512]{2,1,0:T(8,128)(2,1)S(1)}, u32[]{:S(2)}, u32[]{:S(2)}) async-start(bf16[16,40,512]{2,1,0:T(8,128)(2,1)} %bitcast.62), calls=%async_computation.5 | async-start | bytes 1310720 | tf_op jit(solution)/shard_map/all_to_all | solution.py:67
  306.3 0.1 convert_reduce_fusion.1
  306.4 0.5 fusion.10
  306.8 1.1 fusion.5
  308.0 13.9 %psum.7 = f32[128,2]{0,1:T(2,128)} all-reduce(f32[128,2]{0,1:T(2,128)S(1)} %pad_maximum_fusion), channel_id=1, replica_groups=mesh['dp'=16,'fsdp'=8] {'fsdp'}, use_global_device_ids=true, to_apply=%region_9.11 | all-reduce | flops 256 | bytes 2048 | tf_op jit(solution)/shard_map/psum | solution.py:106
  321.9 0.1 convert_reduce_fusion
  322.0 1.1 convolution_convert_fusion.6
  (38 shorter events, 0.3 us)
Async XLA Ops:
  7.2 5.8 %collective-permute-start = (bf16[128,512]{1,0:T(8,128)(2,1)}, bf16[128,512]{1,0:T(8,128)(2,1)S(1)}, u32[]{:S(2)}, u32[]{:S(2)}) collective-permute-start(bf16[128,512]{1,0:T(8,128)(2,1)} %param.9), channel_id=1, source_target_pairs={{0,1},{1,2},{2,3},{3,4},{4,5},{5,6},{6,7},{7,0},{8,9},{9,10},{10,1... | collective-permute-start | bytes 393224 | tf_op jit(solution)/shard_map/ppermute | solution.py:14
  13.0 5.6 %collective-permute-start.1 = (bf16[128,512]{1,0:T(8,128)(2,1)S(1)}, bf16[128,512]{1,0:T(8,128)(2,1)S(1)}, u32[]{:S(2)}, u32[]{:S(2)}) collective-permute-start(bf16[128,512]{1,0:T(8,128)(2,1)S(1)} %collective-permute-done), channel_id=1, source_target_pairs={{0,1},{1,2},{2,3},{3,4},{4,5},{5,6},{6,7},{7,0},{8,9},{9,10},{10,1... | collective-permute-start | bytes 393224 | tf_op jit(solution)/shard_map/ppermute | solution.py:14
  18.6 5.6 %collective-permute-start.2 = (bf16[128,512]{1,0:T(8,128)(2,1)S(1)}, bf16[128,512]{1,0:T(8,128)(2,1)S(1)}, u32[]{:S(2)}, u32[]{:S(2)}) collective-permute-start(bf16[128,512]{1,0:T(8,128)(2,1)S(1)} %collective-permute-done.1), channel_id=1, source_target_pairs={{0,1},{1,2},{2,3},{3,4},{4,5},{5,6},{6,7},{7,0},{8,9},{9,10},{10,1... | collective-permute-start | bytes 393224 | tf_op jit(solution)/shard_map/ppermute | solution.py:14
  24.2 5.6 %collective-permute-start.3 = (bf16[128,512]{1,0:T(8,128)(2,1)S(1)}, bf16[128,512]{1,0:T(8,128)(2,1)S(1)}, u32[]{:S(2)}, u32[]{:S(2)}) collective-permute-start(bf16[128,512]{1,0:T(8,128)(2,1)S(1)} %collective-permute-done.2), channel_id=1, source_target_pairs={{0,1},{1,2},{2,3},{3,4},{4,5},{5,6},{6,7},{7,0},{8,9},{9,10},{10,1... | collective-permute-start | bytes 393224 | tf_op jit(solution)/shard_map/ppermute | solution.py:14
  29.8 5.6 %collective-permute-start.4 = (bf16[128,512]{1,0:T(8,128)(2,1)S(1)}, bf16[128,512]{1,0:T(8,128)(2,1)S(1)}, u32[]{:S(2)}, u32[]{:S(2)}) collective-permute-start(bf16[128,512]{1,0:T(8,128)(2,1)S(1)} %collective-permute-done.3), channel_id=1, source_target_pairs={{0,1},{1,2},{2,3},{3,4},{4,5},{5,6},{6,7},{7,0},{8,9},{9,10},{10,1... | collective-permute-start | bytes 393224 | tf_op jit(solution)/shard_map/ppermute | solution.py:14
  35.4 5.6 %collective-permute-start.5 = (bf16[128,512]{1,0:T(8,128)(2,1)S(1)}, bf16[128,512]{1,0:T(8,128)(2,1)S(1)}, u32[]{:S(2)}, u32[]{:S(2)}) collective-permute-start(bf16[128,512]{1,0:T(8,128)(2,1)S(1)} %collective-permute-done.4), channel_id=1, source_target_pairs={{0,1},{1,2},{2,3},{3,4},{4,5},{5,6},{6,7},{7,0},{8,9},{9,10},{10,1... | collective-permute-start | bytes 393224 | tf_op jit(solution)/shard_map/ppermute | solution.py:14
  41.0 5.6 %collective-permute-start.6 = (bf16[128,512]{1,0:T(8,128)(2,1)S(1)}, bf16[128,512]{1,0:T(8,128)(2,1)S(1)}, u32[]{:S(2)}, u32[]{:S(2)}) collective-permute-start(bf16[128,512]{1,0:T(8,128)(2,1)S(1)} %collective-permute-done.5), channel_id=1, source_target_pairs={{0,1},{1,2},{2,3},{3,4},{4,5},{5,6},{6,7},{7,0},{8,9},{9,10},{10,1... | collective-permute-start | bytes 393224 | tf_op jit(solution)/shard_map/ppermute | solution.py:14
  51.6 8.5 %copy-start = (bf16[128,512]{1,0:T(8,128)(2,1)S(1)}, bf16[128,512]{1,0:T(8,128)(2,1)}, u32[]{:S(2)}) copy-start(bf16[128,512]{1,0:T(8,128)(2,1)} %param.15) | copy-start | bytes 393220
  51.6 42.1 %copy-start.1 = (f32[128,2]{0,1:T(2,128)S(1)}, f32[128,2]{0,1:T(2,128)}, u32[]{:S(2)}) copy-start(f32[128,2]{0,1:T(2,128)} %param.11) | copy-start | bytes 3076
  51.6 68.4 %all-to-all-start = ((bf16[16,40,4096]{2,1,0:T(8,128)(2,1)}), bf16[16,40,4096]{2,1,0:T(8,128)(2,1)}, u32[]{:S(2)}, u32[]{:S(2)}) async-start(bf16[16,40,4096]{2,1,0:T(8,128)(2,1)} %bitcast.55), calls=%async_computation | async-start | bytes 10485760 | tf_op jit(solution)/shard_map/all_to_all | solution.py:58
  60.1 5.6 %collective-permute-start.7 = (bf16[128,512]{1,0:T(8,128)(2,1)S(1)}, bf16[128,512]{1,0:T(8,128)(2,1)S(1)}, u32[]{:S(2)}, u32[]{:S(2)}) collective-permute-start(bf16[128,512]{1,0:T(8,128)(2,1)S(1)} %copy-done), channel_id=1, source_target_pairs={{0,1},{1,2},{2,3},{3,4},{4,5},{5,6},{6,7},{7,0},{8,9},{9,10},{10,1... | collective-permute-start | bytes 393224 | tf_op jit(solution)/shard_map/ppermute | solution.py:14
  65.7 5.6 %collective-permute-start.8 = (bf16[128,512]{1,0:T(8,128)(2,1)S(1)}, bf16[128,512]{1,0:T(8,128)(2,1)S(1)}, u32[]{:S(2)}, u32[]{:S(2)}) collective-permute-start(bf16[128,512]{1,0:T(8,128)(2,1)S(1)} %collective-permute-done.7), channel_id=1, source_target_pairs={{0,1},{1,2},{2,3},{3,4},{4,5},{5,6},{6,7},{7,0},{8,9},{9,10},{10,1... | collective-permute-start | bytes 393224 | tf_op jit(solution)/shard_map/ppermute | solution.py:14
  71.3 5.6 %collective-permute-start.9 = (bf16[128,512]{1,0:T(8,128)(2,1)S(1)}, bf16[128,512]{1,0:T(8,128)(2,1)S(1)}, u32[]{:S(2)}, u32[]{:S(2)}) collective-permute-start(bf16[128,512]{1,0:T(8,128)(2,1)S(1)} %collective-permute-done.8), channel_id=1, source_target_pairs={{0,1},{1,2},{2,3},{3,4},{4,5},{5,6},{6,7},{7,0},{8,9},{9,10},{10,1... | collective-permute-start | bytes 393224 | tf_op jit(solution)/shard_map/ppermute | solution.py:14
  76.9 5.6 %collective-permute-start.10 = (bf16[128,512]{1,0:T(8,128)(2,1)S(1)}, bf16[128,512]{1,0:T(8,128)(2,1)S(1)}, u32[]{:S(2)}, u32[]{:S(2)}) collective-permute-start(bf16[128,512]{1,0:T(8,128)(2,1)S(1)} %collective-permute-done.9), channel_id=1, source_target_pairs={{0,1},{1,2},{2,3},{3,4},{4,5},{5,6},{6,7},{7,0},{8,9},{9,10},{10,1... | collective-permute-start | bytes 393224 | tf_op jit(solution)/shard_map/ppermute | solution.py:14
  82.5 5.6 %collective-permute-start.11 = (bf16[128,512]{1,0:T(8,128)(2,1)S(1)}, bf16[128,512]{1,0:T(8,128)(2,1)S(1)}, u32[]{:S(2)}, u32[]{:S(2)}) collective-permute-start(bf16[128,512]{1,0:T(8,128)(2,1)S(1)} %collective-permute-done.10), channel_id=1, source_target_pairs={{0,1},{1,2},{2,3},{3,4},{4,5},{5,6},{6,7},{7,0},{8,9},{9,10},{10,1... | collective-permute-start | bytes 393224 | tf_op jit(solution)/shard_map/ppermute | solution.py:14
  88.1 5.6 %collective-permute-start.12 = (bf16[128,512]{1,0:T(8,128)(2,1)S(1)}, bf16[128,512]{1,0:T(8,128)(2,1)S(1)}, u32[]{:S(2)}, u32[]{:S(2)}) collective-permute-start(bf16[128,512]{1,0:T(8,128)(2,1)S(1)} %collective-permute-done.11), channel_id=1, source_target_pairs={{0,1},{1,2},{2,3},{3,4},{4,5},{5,6},{6,7},{7,0},{8,9},{9,10},{10,1... | collective-permute-start | bytes 393224 | tf_op jit(solution)/shard_map/ppermute | solution.py:14
  93.7 5.6 %collective-permute-start.13 = (bf16[128,512]{1,0:T(8,128)(2,1)S(1)}, bf16[128,512]{1,0:T(8,128)(2,1)S(1)}, u32[]{:S(2)}, u32[]{:S(2)}) collective-permute-start(bf16[128,512]{1,0:T(8,128)(2,1)S(1)} %collective-permute-done.12), channel_id=1, source_target_pairs={{0,1},{1,2},{2,3},{3,4},{4,5},{5,6},{6,7},{7,0},{8,9},{9,10},{10,1... | collective-permute-start | bytes 393224 | tf_op jit(solution)/shard_map/ppermute | solution.py:14
  123.0 69.4 %all-to-all-start.2 = ((bf16[16,40,4096]{2,1,0:T(8,128)(2,1)}), bf16[16,40,4096]{2,1,0:T(8,128)(2,1)}, u32[]{:S(2)}, u32[]{:S(2)}) async-start(bf16[16,40,4096]{2,1,0:T(8,128)(2,1)} %bitcast.56), calls=%async_computation.3 | async-start | bytes 10485760 | tf_op jit(solution)/shard_map/all_to_all | solution.py:58
  131.6 125.5 %reduce-scatter.3.cloned.1.call-start = ((), (), s32[]{:S(2)}) async-start(), calls=%async_computation.6 | async-start | bytes 5898240 | tf_op jit(solution)/shard_map/reduce_scatter | solution.py:64
  131.8 7.8 %copy-start.3 = (bf16[4096,512]{1,0:T(8,128)(2,1)S(1)}, bf16[4096,512]{1,0:T(8,128)(2,1)}, u32[]{:S(2)}) copy-start(bf16[4096,512]{1,0:T(8,128)(2,1)} %param.13) | copy-start | bytes 12582916
  192.3 8.0 %copy-start.2 = (bf16[512,4096]{1,0:T(8,128)(2,1)S(1)}, bf16[512,4096]{1,0:T(8,128)(2,1)}, u32[]{:S(2)}) copy-start(bf16[512,4096]{1,0:T(8,128)(2,1)} %param.14) | copy-start | bytes 12582916
  205.0 93.8 %reduce-scatter.5.cloned.1.call-start = ((), (), s32[]{:S(2)}) async-start(), calls=%async_computation.7 | async-start | bytes 5898240 | tf_op jit(solution)/shard_map/reduce_scatter | solution.py:64
  205.3 4.9 %copy-start.4 = (bf16[4096,512]{1,0:T(8,128)(2,1)S(1)}, bf16[4096,512]{1,0:T(8,128)(2,1)}, u32[]{:S(2)}) copy-start(bf16[4096,512]{1,0:T(8,128)(2,1)} %param.13) | copy-start | bytes 12582916
  257.0 41.8 %all-to-all-start.1 = ((bf16[16,40,512]{2,1,0:T(8,128)(2,1)}), bf16[16,40,512]{2,1,0:T(8,128)(2,1)S(1)}, u32[]{:S(2)}, u32[]{:S(2)}) async-start(bf16[16,40,512]{2,1,0:T(8,128)(2,1)} %bitcast.63), calls=%async_computation.2 | async-start | bytes 1310720 | tf_op jit(solution)/shard_map/all_to_all | solution.py:67
  298.9 23.0 %all-to-all-start.3 = ((bf16[16,40,512]{2,1,0:T(8,128)(2,1)}), bf16[16,40,512]{2,1,0:T(8,128)(2,1)S(1)}, u32[]{:S(2)}, u32[]{:S(2)}) async-start(bf16[16,40,512]{2,1,0:T(8,128)(2,1)} %bitcast.62), calls=%async_computation.5 | async-start | bytes 1310720 | tf_op jit(solution)/shard_map/all_to_all | solution.py:67
Sparse Core Ops, SparseCore 0:
  205.2 51.8 reduce-scatter.2
  259.4 39.3 reduce-scatter.4
